TPU v7x, 512 devices: a whole 4x8x8 slice. The times are simulated.
512 devices in a mesh: req: 64 (over z, x, core), tp: 8 (over y).
Axes of the slice: x: 4, y: 8, z: 8, core: 2. Of those that a mesh axis runs over, the one named last changes fastest.
Arguments:
- queries: bfloat16 [1024, 2048], P('req', 'tp'), may hold values from -27 to 27
- fresh_cache: bfloat16 [1024, 2, 2048], P('req', None, 'tp'), may hold values from -4 to 4
- tail_cache: bfloat16 [1024, 32, 2, 2048], P('req', None, None, 'tp'), may hold values from -4 to 4
- tail_len: int32 [1024], P('req'), may hold values from 1 to 32, as said below
- pool_cache: bfloat16 [2048, 64, 2, 2048], P('req', None, None, 'tp'), may hold values from -4 to 4
- page_group: int32 [2048], P('req'), may hold values from 0 to 63, as said below
- page_start: int32 [2048], P('req'), may hold values from 0 to 16320, as said below
- prompt_len: int32 [64], replicated, may hold values from 1 to 16384, as said below
- residual: bfloat16 [1024, 2048], P('req'), may hold values from -80 to 80
- out_weight: bfloat16 [2048, 2048], P('tp'), may hold values from -0.125 to 0.125
- out_bias: bfloat16 [2048], replicated, may hold values from -0.796875 to 0.796875
- norm_gain: bfloat16 [2048], P('tp'), may hold values from 0.5 to 1.5
- norm_shift: bfloat16 [2048], P('tp'), may hold values from -0.796875 to 0.796875
Outputs:
- attention_out: bfloat16 [1024, 2048], P('req', 'tp')
- normed: bfloat16 [1024, 2048], P('req', 'tp')
Inputs may be any that keep to these rules, and one draw needn't show every extreme that they name: page_group[p] is the group whose prompt page p holds; every page holds some group's prompt; every group holds at least one page and at most 256 pages, and some group holds exactly 256; the pages of a group of n pages lie on min(n, 64) different indices of req, none holding more than ceil(n / 64) of them. The pages of a group of n pages have page_start 0, 64, ..., (n - 1) * 64, each once. `prompt_len`: a group of n pages has a prompt of (n - 1) * 64 + 1 to n * 64 positions. `tail_len`: some request has exactly 32 tail positions.
All inputs are finite; a program needn't handle non-finite values.
Results may differ from a plain program's by a relative error of at most 0.02.
Values may be sent and summed in bfloat16 or wider, within the bound.
No kernel may reach another device: no remote copies, remote signals or barrier semaphores. Data moves between devices by JAX's collectives and lax.ppermute only.
A program may use at most 64 MiB of HBM per device.

v0:
```python
import math
import jax
import jax.numpy as jnp
from jax import lax
from jax.sharding import PartitionSpec as P

HEADS = 16
HEAD = 128
PAGE = 64
masked_score = -1e30
norm_epsilon = 1e-05


def split_halves(values):
    upper_part = lax.optimization_barrier(values.astype(jnp.bfloat16))
    lower_part = (values - upper_part.astype(jnp.float32)).astype(jnp.bfloat16)
    return (upper_part, lower_part)


def local(
    queries,
    fresh_cache,
    tail_cache,
    tail_len,
    pool_cache,
    page_group,
    page_start,
    prompt_len,
    residual,
    out_weight,
    out_bias,
    norm_gain,
    norm_shift,
):
    f32 = jnp.float32
    highest = lax.Precision.HIGHEST
    row_count, feat_width = queries.shape
    heads_here = feat_width // HEAD
    inv_root = 1.0 / math.sqrt(HEAD)
    head_ids = lax.axis_index("tp") * heads_here + jnp.arange(heads_here)
    slopes = jnp.exp2(-8.0 * (head_ids.astype(f32) + 1.0) / HEADS)
    group_count = prompt_len.shape[0]
    page_count = pool_cache.shape[0]
    tail_slots = tail_cache.shape[1]
    req_index = lax.axis_index("req")
    everyone = lax.all_gather(queries, "req", axis=0, tiled=True)
    by_group = everyone.reshape(group_count, row_count, heads_here, HEAD)
    safe_group = jnp.clip(page_group, 0, group_count - 1)
    page_queries = by_group[safe_group]
    page_keys = pool_cache[:, :, 0].reshape(page_count, PAGE, heads_here, HEAD)
    page_values = pool_cache[:, :, 1].reshape(page_count, PAGE, heads_here, HEAD)
    prompt_here = prompt_len[safe_group]
    positions = page_start[:, None] + jnp.arange(PAGE)[None, :]
    usable = (positions < prompt_here[:, None]) & (page_group[:, None] >= 0)
    offsets = (positions - prompt_here[:, None]).astype(f32)
    scores = (
        jnp.einsum("pqhd,pshd->pqhs", page_queries, page_keys, preferred_element_type=f32)
        * inv_root
    )
    scores = scores + slopes[None, None, :, None] * offsets[:, None, None, :]
    scores = jnp.where(usable[:, None, None, :], scores, masked_score)
    member = page_group[:, None] == jnp.arange(group_count)[None, :]
    page_top = scores.max(-1)
    group_top = jnp.where(member[:, :, None, None], page_top[:, None], masked_score).max(0)
    group_top = group_top.reshape(group_count * row_count, heads_here)
    home_queries = queries.reshape(row_count, heads_here, HEAD)
    tail_keys = tail_cache[:, :, 0].reshape(row_count, tail_slots, heads_here, HEAD)
    tail_values = tail_cache[:, :, 1].reshape(row_count, tail_slots, heads_here, HEAD)
    fresh_keys = fresh_cache[:, 0].reshape(row_count, heads_here, HEAD)
    fresh_values = fresh_cache[:, 1].reshape(row_count, heads_here, HEAD)
    slot_ids = jnp.arange(tail_slots)
    tail_scores = (
        jnp.einsum("qhd,qjhd->qhj", home_queries, tail_keys, preferred_element_type=f32) * inv_root
    )
    tail_scores = tail_scores + slopes[None, :, None] * slot_ids.astype(f32)[None, None, :]
    tail_scores = jnp.where(
        slot_ids[None, None, :] < tail_len[:, None, None], tail_scores, masked_score
    )
    own_scores = (
        jnp.einsum("qhd,qhd->qh", home_queries, fresh_keys, preferred_element_type=f32) * inv_root
    )
    own_scores = own_scores + slopes[None, :] * tail_len.astype(f32)[:, None]
    home_top = jnp.maximum(tail_scores.max(-1), own_scores)
    mine = lax.dynamic_slice_in_dim(group_top, req_index * row_count, row_count, 0)
    merged = lax.dynamic_update_slice_in_dim(
        group_top, jnp.maximum(mine, home_top), req_index * row_count, 0
    )
    all_top = lax.pmax(merged, "req")
    reference_top = all_top.reshape(group_count, row_count, heads_here)[safe_group]
    weights = jnp.where(usable[:, None, None, :], jnp.exp(scores - reference_top[..., None]), 0.0)
    page_totals = weights.sum(-1)
    upper_part, lower_part = split_halves(weights)
    page_accum = jnp.einsum("pqhs,pshd->pqhd", upper_part, page_values, preferred_element_type=f32)
    page_accum = page_accum + jnp.einsum(
        "pqhs,pshd->pqhd", lower_part, page_values, preferred_element_type=f32
    )
    accum_upper, accum_lower = split_halves(page_accum.reshape(page_count, -1))
    spread = member.T.astype(jnp.bfloat16)
    accum = jnp.dot(spread, accum_upper, preferred_element_type=f32)
    accum = accum + jnp.dot(spread, accum_lower, preferred_element_type=f32)
    totals = jnp.dot(member.T.astype(f32), page_totals.reshape(page_count, -1), precision=highest)
    totals, accum = (
        totals.reshape(group_count * row_count, heads_here),
        accum.reshape(group_count * row_count, feat_width),
    )
    pool_totals, pool_accum = (
        lax.psum_scatter(totals, "req", scatter_dimension=0, tiled=True),
        lax.psum_scatter(accum, "req", scatter_dimension=0, tiled=True),
    )
    pool_accum = pool_accum.reshape(row_count, heads_here, HEAD)
    row_top = lax.dynamic_slice_in_dim(all_top, req_index * row_count, row_count, 0)
    tail_weights = jnp.exp(tail_scores - row_top[:, :, None])
    own_weights = jnp.exp(own_scores - row_top)
    totals = tail_weights.sum(-1) + own_weights
    upper_part, lower_part = split_halves(tail_weights)
    accum = jnp.einsum("qhj,qjhd->qhd", upper_part, tail_values, preferred_element_type=f32)
    accum = accum + jnp.einsum("qhj,qjhd->qhd", lower_part, tail_values, preferred_element_type=f32)
    home_accum = accum + own_weights[:, :, None] * fresh_values.astype(f32)
    attention = ((pool_accum + home_accum) / (pool_totals + totals)[:, :, None]).astype(
        jnp.bfloat16
    )
    attention = attention.reshape(row_count, feat_width)
    partial_value = jnp.dot(attention, out_weight, preferred_element_type=f32)
    model_width = residual.shape[1]
    own_start = lax.axis_index("tp") * feat_width
    summed = lax.psum_scatter(
        partial_value.astype(jnp.bfloat16), "tp", scatter_dimension=1, tiled=True
    ).astype(jnp.float32)
    bias_mine = lax.dynamic_slice_in_dim(out_bias, own_start, feat_width, 0).astype(f32)
    attention_mine = (summed + bias_mine[None, :]).astype(jnp.bfloat16)
    residual_mine = lax.dynamic_slice_in_dim(residual, own_start, feat_width, 1).astype(f32)
    hidden_mine = residual_mine + attention_mine.astype(f32)
    first_sum, second_sum = lax.psum(
        (jnp.sum(hidden_mine, -1), jnp.sum(hidden_mine * hidden_mine, -1)), "tp"
    )
    row_mean = (first_sum / model_width)[:, None]
    mean_square = (second_sum / model_width)[:, None]
    row_var = mean_square - row_mean * row_mean
    normed = (
        (hidden_mine - row_mean)
        * lax.rsqrt(row_var + norm_epsilon)
        * norm_gain.astype(f32)[None, :]
    )
    normed = normed + norm_shift.astype(f32)[None, :]
    return (attention_mine, normed.astype(jnp.bfloat16))


def solution(mesh):
    in_specs = (
        P("req", "tp"),
        P("req", None, "tp"),
        P("req", None, None, "tp"),
        P("req"),
        P("req", None, None, "tp"),
        P("req"),
        P("req"),
        P(),
        P("req", None),
        P("tp", None),
        P(),
        P("tp"),
        P("tp"),
    )
    out_specs = (P("req", "tp"), P("req", "tp"))
    return jax.shard_map(local, mesh=mesh, in_specs=in_specs, out_specs=out_specs, check_vma=False)
```

profile of v0, /device:TPU:2, one launch (start us, length us, event | category | flops | bytes accessed | tf_op | source)
XLA Modules:
  0.0 536.2 jit_solution(4596948644088355456)
XLA Ops:
  7.2 0.7 compare_select_fusion
  8.0 0.7 broadcast_compare_fusion
  8.6 0.7 iota_compare_fusion
  9.4 56.0 %all_gather.3 = bf16[1024,256]{1,0:T(8,128)(2,1)S(1)} all-gather(bf16[16,256]{1,0:T(8,128)(2,1)} %param.13), channel_id=1, replica_groups=mesh['req'=64,'tp'=8] {'req'}, dimensions={0}, use_global_device_ids=true | all-gather | bytes 532480 | tf_op jit(solution)/shard_map/all_gather | solution.py:46
  65.4 0.7 reshape.271
  66.1 0.7 reshape.226
  66.8 0.7 iota_compare_fusion.3
  67.5 0.7 convert_element_type.100
  68.2 1.4 gather_fusion
  69.5 0.7 subtract_convert_fusion.5
  70.3 0.7 fusion.31
  71.2 0.6 gather_fusion.1
  71.8 10.7 %slice_reduce_fusion = (bf16[32,64,256]{2,1,0:T(8,128)(2,1)S(1)}, bf16[32,64,256]{2,1,0:T(8,128)(2,1)S(1)}) fusion(bf16[32,64,2,256]{3,2,1,0:T(2,128)(2,1)} %param.17), kind=kLoop, calls=%fused_computation.5 | loop fusion | bytes 4194304 | tf_op jit(solution)/shard_map/slice | solution.py:51
  82.6 0.8 fusion.48
  83.9 2.9 slice_reduce_fusion.2
  87.0 1.2 fusion.17
  88.6 124.1 %pmax.7 = f32[1024,2]{0,1:T(2,128)S(1)} all-reduce(f32[1024,2]{0,1:T(2,128)S(1)} %dynamic_update_slice.3), channel_id=1, replica_groups=mesh['req'=64,'tp'=8] {'req'}, use_global_device_ids=true, to_apply=%region_3.4 | all-reduce | flops 2048 | bytes 16384 | tf_op jit(solution)/shard_map/pmax | solution.py:88
  212.8 0.6 gather_fusion.2
  213.4 0.4 fusion.11
  214.2 0.5 fusion
  215.0 0.4 reshape.228
  215.9 0.4 convolution_add_fusion
  216.3 1.1 reshape.229
  218.4 1.3 dynamic-slice
  220.3 249.1 %all-reduce = f32[1024,2]{1,0:T(8,128)S(1)} all-reduce(f32[1024,2]{1,0:T(8,128)S(1)} %reshape.232), channel_id=3, replica_groups=mesh['req'=64,'tp'=8] {'req'}, use_global_device_ids=true, to_apply=%region_6.7.clone | all-reduce | flops 2048 | bytes 16384
  470.4 0.7 reshape.230
  471.2 0.9 convolution_convert_fusion
  472.2 0.8 dynamic-slice_convert_fusion
  472.9 38.6 %reduce-scatter.5.cloned.1.call-done = bf16[16,256]{1,0:T(8,128)(2,1)} async-done(((bf16[16,2048]{1,0:T(8,128)(2,1)}), bf16[16,256]{1,0:T(8,128)(2,1)}) %reduce-scatter.5.cloned.1.call-update) | async-done | bytes 8208 | tf_op jit(solution)/shard_map/reduce_scatter | solution.py:126
  511.6 0.8 fusion.33
  512.4 15.6 %all-reduce.1 = (f32[16]{0:T(128)S(1)}, f32[16]{0:T(128)S(1)}) all-reduce(f32[16]{0:T(128)S(1)} %get-tuple-element.7, f32[16]{0:T(128)S(1)} %get-tuple-element.6), channel_id=1, replica_groups=mesh['req'=64,'tp'=8] {'tp'}, use_global_device_ids=true, to_apply=%region_12.13 | all-reduce | flops 32 | bytes 256 | tf_op jit(solution)/shard_map/psum | solution.py:133
  528.0 1.4 add_convert_fusion
  (59 shorter events, 4.6 us)
Async XLA Ops:
  7.2 464.0 %copy-start = (bf16[256,2048]{1,0:T(8,128)(2,1)S(1)}, bf16[256,2048]{1,0:T(8,128)(2,1)}, u32[]{:S(2)}) copy-start(bf16[256,2048]{1,0:T(8,128)(2,1)} %param.22) | copy-start | bytes 3145732
  7.2 463.2 %reduce-scatter.3.cloned.1.call-start = ((), (), s32[]{:S(2)}) async-start(), calls=%async_computation.2 | async-start | bytes 1064960 | tf_op jit(solution)/shard_map/reduce_scatter | solution.py:108
  82.5 1.3 copy-start.1
  82.5 4.2 copy-start.2
  214.7 0.8 copy-start.4
  217.5 254.6 %copy-start.5 = (bf16[256]{0:T(256)(128)(2,1)S(1)}, bf16[256]{0:T(256)(128)(2,1)}, u32[]{:S(2)}) copy-start(bf16[256]{0:T(256)(128)(2,1)} %param.24) | copy-start | bytes 1540
  217.5 254.6 %copy-start.6 = (bf16[256]{0:T(256)(128)(2,1)S(1)}, bf16[256]{0:T(256)(128)(2,1)}, u32[]{:S(2)}) copy-start(bf16[256]{0:T(256)(128)(2,1)} %param.25) | copy-start | bytes 1540
  217.5 294.0 %reduce-scatter.5.cloned.1.call-start = ((), (), s32[]{:S(2)}) async-start(), calls=%async_computation.3 | async-start | bytes 73728 | tf_op jit(solution)/shard_map/reduce_scatter | solution.py:126
  512.4 17.0 %copy-start.3 = (bf16[16,256]{1,0:T(8,128)(2,1)}, bf16[16,256]{1,0:T(8,128)(2,1)S(1)}, u32[]{:S(2)}) copy-start(bf16[16,256]{1,0:T(8,128)(2,1)S(1)} %get-tuple-element.10) | copy-start | bytes 24580
Sparse Core Ops, SparseCore 0:
  217.6 148.1 reduce-scatter.2
  472.2 39.2 reduce-scatter.4
where the time goes:
time: 537 us; the launch traced here: 536 us
  blocking collectives  445 us (83%)
  waiting for transfers between devices  38.7 us (7%)
  local copies, waits for them, and re-layouts  22.9 us (4%)
  between operations  15 us (3%)
  other arithmetic  9.58 us (2%)
    unnamed x1, blocking collectives  249 us
    pmax x1, blocking collectives, local(): all_top = lax.pmax(merged, 'req')  124 us
    all_gather x1, blocking collectives, local(): everyone = lax.all_gather(queries, 'req', axis=0, tiled=True)  56 us
    reduce_scatter x1, waiting for transfers between devices, local(): lax.psum_scatter(partial_value.astype(jnp.bfloat16), 'tp', scatter_dimens...  38.6 us
    psum x1, blocking collectives, local(): lax.psum((jnp.sum(hidden_mine, -1), jnp.sum(hidden_mine * hidden_mine, -1...  15.6 us
  transfers between devices with their start and end apart: 2, of which 1 were waited for; matrix products, arithmetic and copies ran while one was open for 1% of the time, Pallas kernels for 0%

commit v1 on v0

--- a/solution.py
+++ b/solution.py
@@ -43,7 +43,9 @@
     page_count = pool_cache.shape[0]
     tail_slots = tail_cache.shape[1]
     req_index = lax.axis_index("req")
-    everyone = lax.all_gather(queries, "req", axis=0, tiled=True)
+    everyone = jnp.concatenate(
+        lax.all_to_all(jnp.stack([queries] * lax.axis_size("req")), "req", 0, 0), axis=0
+    )
     by_group = everyone.reshape(group_count, row_count, heads_here, HEAD)
     safe_group = jnp.clip(page_group, 0, group_count - 1)
     page_queries = by_group[safe_group]

time: 537 us -> 497 us (0.926)
  blocking collectives: 445 us -> 391 us
  starting transfers between devices: 0.08 us -> 13.9 us
    all_gather x1 -> x0, blocking collectives: 56 us -> none  [local(): everyone = lax.all_gather(queries, 'req', axis=0, tiled=True)]
    all_to_all x0 -> x1, starting transfers between devices: none -> 13.9 us  [local(): lax.all_to_all(jnp.stack([queries] * lax.axis_size('req')), 'req', 0, 0)]
  transfers between devices with their start and end apart: 2 -> 3, of which waited for: 1 -> 1; matrix products, arithmetic and copies ran while one was open for 1% -> 5% of each run, Pallas kernels for 0% -> 0%
where the time goes in v1:
time: 497 us
  blocking collectives  391 us (79%)
  waiting for transfers between devices  39.4 us (8%)
  local copies, waits for them, and re-layouts  25.4 us (5%)
  between operations  15 us (3%)
  starting transfers between devices  13.9 us (3%)
  other arithmetic  6.86 us (1%)
  matrix products  5.46 us (1%)
    unnamed x1, blocking collectives  249 us
    pmax x1, blocking collectives, local(): all_top = lax.pmax(merged, 'req')  126 us
    reduce_scatter x1, waiting for transfers between devices, local(): lax.psum_scatter(partial_value.astype(jnp.bfloat16), 'tp', scatter_dimens...  39.3 us
    psum x1, blocking collectives, local(): lax.psum((jnp.sum(hidden_mine, -1), jnp.sum(hidden_mine * hidden_mine, -1...  15.6 us
    all_to_all x1, starting transfers between devices, local(): lax.all_to_all(jnp.stack([queries] * lax.axis_size('req')), 'req', 0, 0)  13.9 us
    slice x1, local copies, waits for them, and re-layouts, local(): pool_cache[:, :, 1].reshape(page_count, PAGE, heads_here, HEAD)  11.7 us
  transfers between devices with their start and end apart: 3, of which 1 were waited for; matrix products, arithmetic and copies ran while one was open for 5% of the time, Pallas kernels for 0%

profile of v1, /device:TPU:2, one launch (start us, length us, event | category | flops | bytes accessed | tf_op | source)
XLA Modules:
  0.0 496.7 jit_solution(17686075630075350942)
XLA Ops:
  7.2 1.7 stack.2
  8.9 13.9 %all-to-all-start = ((bf16[64,16,256]{2,1,0:T(8,128)(2,1)}), bf16[64,16,256]{2,1,0:T(8,128)(2,1)S(1)}, u32[]{:S(2)}, u32[]{:S(2)}) async-start(bf16[64,16,256]{2,1,0:T(8,128)(2,1)} %stack.2), calls=%async_computation | async-start | bytes 1048576 | tf_op jit(solution)/shard_map/all_to_all | solution.py:47
  22.8 0.7 compare_select_fusion
  23.5 0.7 broadcast_compare_fusion
  24.1 0.7 iota_compare_fusion
  24.9 0.7 reshape.269
  25.6 0.7 reshape.224
  26.3 1.4 gather_fusion
  27.8 2.8 slice_reduce_fusion.2
  31.5 11.7 %slice_reduce_fusion = (bf16[32,64,256]{2,1,0:T(8,128)(2,1)S(1)}, bf16[32,64,256]{2,1,0:T(8,128)(2,1)}) fusion(bf16[32,64,2,256]{3,2,1,0:T(2,128)(2,1)} %param.17), kind=kLoop, calls=%fused_computation.5 | loop fusion | bytes 4194304 | tf_op jit(solution)/shard_map/slice | solution.py:53
  43.3 0.6 gather_fusion.1
  43.9 2.0 fusion.48
  46.5 125.9 %pmax.7 = f32[1024,2]{0,1:T(2,128)S(1)} all-reduce(f32[1024,2]{0,1:T(2,128)S(1)} %dynamic_update_slice.3), channel_id=1, replica_groups=mesh['req'=64,'tp'=8] {'req'}, use_global_device_ids=true, to_apply=%region_3.4 | all-reduce | flops 2048 | bytes 16384 | tf_op jit(solution)/shard_map/pmax | solution.py:90
  172.5 0.6 gather_fusion.2
  173.2 0.4 fusion.11
  173.6 0.4 fusion.5
  174.0 0.5 fusion
  174.8 0.4 reshape.226
  175.2 0.4 fusion.35
  175.7 0.4 convolution_add_fusion
  176.1 1.1 reshape.227
  177.3 1.3 dynamic-slice
  179.5 0.3 fusion.38
  179.8 0.3 reshape.230
  180.1 249.1 %all-reduce = f32[1024,2]{1,0:T(8,128)S(1)} all-reduce(f32[1024,2]{1,0:T(8,128)S(1)} %reshape.230), channel_id=3, replica_groups=mesh['req'=64,'tp'=8] {'req'}, use_global_device_ids=true, to_apply=%region_6.7.clone | all-reduce | flops 2048 | bytes 16384
  430.1 0.7 reshape.228
  431.0 0.9 convolution_convert_fusion
  431.9 0.8 dynamic-slice_convert_fusion
  432.7 39.3 %reduce-scatter.5.cloned.1.call-done = bf16[16,256]{1,0:T(8,128)(2,1)} async-done(((bf16[16,2048]{1,0:T(8,128)(2,1)}), bf16[16,256]{1,0:T(8,128)(2,1)}) %reduce-scatter.5.cloned.1.call-update) | async-done | bytes 8208 | tf_op jit(solution)/shard_map/reduce_scatter | solution.py:128
  472.0 0.8 fusion.33
  472.8 15.6 %all-reduce.1 = (f32[16]{0:T(128)S(1)}, f32[16]{0:T(128)S(1)}) all-reduce(f32[16]{0:T(128)S(1)} %get-tuple-element.7, f32[16]{0:T(128)S(1)} %get-tuple-element.6), channel_id=1, replica_groups=mesh['req'=64,'tp'=8] {'tp'}, use_global_device_ids=true, to_apply=%region_12.13 | all-reduce | flops 32 | bytes 256 | tf_op jit(solution)/shard_map/psum | solution.py:135
  488.4 1.4 add_convert_fusion
  (66 shorter events, 3.6 us)
Async XLA Ops:
  7.2 423.8 %copy-start = (bf16[256,2048]{1,0:T(8,128)(2,1)S(1)}, bf16[256,2048]{1,0:T(8,128)(2,1)}, u32[]{:S(2)}) copy-start(bf16[256,2048]{1,0:T(8,128)(2,1)} %param.22) | copy-start | bytes 3145732
  7.2 20.5 %copy-start.6 = (s32[32]{0:T(128)S(1)}, s32[32]{0:T(128)}, u32[]{:S(2)}) copy-start(s32[32]{0:T(128)} %param.19) | copy-start | bytes 388
  7.2 20.6 %copy-start.1 = (bf16[16,32,2,256]{3,2,1,0:T(2,128)(2,1)S(1)}, bf16[16,32,2,256]{3,2,1,0:T(2,128)(2,1)}, u32[]{:S(2)}) copy-start(bf16[16,32,2,256]{3,2,1,0:T(2,128)(2,1)} %param.15) | copy-start | bytes 1572868
  7.2 23.5 %copy-start.7 = (s32[16]{0:T(128)S(1)}, s32[16]{0:T(128)}, u32[]{:S(2)}) copy-start(s32[16]{0:T(128)} %param.16) | copy-start | bytes 196
  7.2 23.5 %copy-start.3 = (bf16[16,2,256]{2,1,0:T(2,128)(2,1)S(1)}, bf16[16,2,256]{2,1,0:T(2,128)(2,1)}, u32[]{:S(2)}) copy-start(bf16[16,2,256]{2,1,0:T(2,128)(2,1)} %param.14) | copy-start | bytes 49156
  8.9 34.3 %all-to-all-start = ((bf16[64,16,256]{2,1,0:T(8,128)(2,1)}), bf16[64,16,256]{2,1,0:T(8,128)(2,1)S(1)}, u32[]{:S(2)}, u32[]{:S(2)}) async-start(bf16[64,16,256]{2,1,0:T(8,128)(2,1)} %stack.2), calls=%async_computation | async-start | bytes 1048576 | tf_op jit(solution)/shard_map/all_to_all | solution.py:47
  22.8 407.4 %reduce-scatter.3.cloned.1.call-start = ((), (), s32[]{:S(2)}) async-start(), calls=%async_computation.3 | async-start | bytes 1064960 | tf_op jit(solution)/shard_map/reduce_scatter | solution.py:110
  174.5 0.8 copy-start.5
  176.1 253.7 %copy-start.2 = (bf16[16,32,256]{2,1,0:T(8,128)(2,1)S(1)}, bf16[16,32,256]{2,1,0:T(8,128)(2,1)}, u32[]{:S(2)}) copy-start(bf16[16,32,256]{2,1,0:T(8,128)(2,1)} %get-tuple-element.4) | copy-start | bytes 786436
  177.3 254.6 %copy-start.8 = (bf16[256]{0:T(256)(128)(2,1)S(1)}, bf16[256]{0:T(256)(128)(2,1)}, u32[]{:S(2)}) copy-start(bf16[256]{0:T(256)(128)(2,1)} %param.24) | copy-start | bytes 1540
  177.3 254.6 %copy-start.9 = (bf16[256]{0:T(256)(128)(2,1)S(1)}, bf16[256]{0:T(256)(128)(2,1)}, u32[]{:S(2)}) copy-start(bf16[256]{0:T(256)(128)(2,1)} %param.25) | copy-start | bytes 1540
  177.3 294.7 %reduce-scatter.5.cloned.1.call-start = ((), (), s32[]{:S(2)}) async-start(), calls=%async_computation.4 | async-start | bytes 73728 | tf_op jit(solution)/shard_map/reduce_scatter | solution.py:128
  472.8 17.0 %copy-start.4 = (bf16[16,256]{1,0:T(8,128)(2,1)}, bf16[16,256]{1,0:T(8,128)(2,1)S(1)}, u32[]{:S(2)}) copy-start(bf16[16,256]{1,0:T(8,128)(2,1)S(1)} %get-tuple-element.10) | copy-start | bytes 24580
Sparse Core Ops, SparseCore 0:
  177.4 148.7 reduce-scatter.2
  432.0 39.9 reduce-scatter.4
